TPU v7x, 32 devices: a whole 2x2x4 slice. The times are simulated.
32 devices in a mesh: narrow: 4 (over y, core), wide: 8 (over z, x).
Axes of the slice: x: 2, y: 2, z: 4, core: 2. Of those that a mesh axis runs over, the one named last changes fastest.
Arguments:
- hidden_in: bfloat16 [256, 16384], P('narrow', 'wide'), may hold values from -6 to 6
- w_query: bfloat16 [16384, 8, 2048], P('wide', 'narrow'), may hold values from -0.046875 to 0.046875
- w_keyval: bfloat16 [16384, 8, 256], P('wide', 'narrow'), may hold values from -0.046875 to 0.046875
- w_out: bfloat16 [16384, 16384], P('narrow', 'wide'), may hold values from -0.125 to 0.125
- key_cache: bfloat16 [256, 8, 1024, 128], P('wide', 'narrow'), may hold values from -1300 to 1300
- value_cache: bfloat16 [256, 8, 1024, 128], P('wide', 'narrow'), may hold values from -6 to 6
- lengths: int32 [256], P('wide'), may hold values from 2 to 1024, as said below
Outputs:
- hidden_out: bfloat16 [256, 16384], P('narrow', 'wide')
Inputs may be any that keep to these rules, and one draw needn't show every extreme that they name: `lengths`: each row holds at least 2 cached tokens; some row holds exactly 1024.
All inputs are finite; a program needn't handle non-finite values.
Results may differ from a plain program's by a relative error of at most 0.019.
The roundings to bfloat16 on the way count: a program that leaves them out, or rounds other values in their place, can miss the bound.
Values may be sent and summed in bfloat16 or wider, within the bound.
No kernel may reach another device: no remote copies, remote signals or barrier semaphores. Data moves between devices by JAX's collectives and lax.ppermute only.
A program may use at most 192 MiB of HBM per device.

v0:
```python
import jax
import jax.numpy as jnp
from jax import lax
from jax.sharding import PartitionSpec as P

STEPS = 2
rope_base = 500000.0


def rope(values, position):
    half = values.shape[-1] // 2
    freq = rope_base ** (-2.0 * jnp.arange(half, dtype=jnp.float32) / values.shape[-1])
    angle = position.astype(jnp.float32)[:, None] * freq[None, :]
    shape = (angle.shape[0],) + (1,) * (values.ndim - 2) + (half,)
    cosine = jnp.cos(angle).reshape(shape)
    sine = jnp.sin(angle).reshape(shape)
    first = values[..., :half]
    second = values[..., half:]
    return jnp.concatenate(
        (first * cosine - second * sine, second * cosine + first * sine), axis=-1
    )


def attend_step(
    every, step, w_q2, w_kv2, w_out, key_cache, value_cache, lengths, new_keys, new_vals
):
    local_rows = key_cache.shape[0]
    groups = key_cache.shape[1]
    slots = key_cache.shape[2]
    head_dim = key_cache.shape[3]
    qcols = w_q2.shape[1]
    per_group = qcols // (groups * head_dim)
    part_q = jnp.dot(every, w_q2, preferred_element_type=jnp.float32)
    part_kv = jnp.dot(every, w_kv2, preferred_element_type=jnp.float32)
    proj = lax.psum_scatter(
        jnp.concatenate((part_q, part_kv), axis=1), "wide", scatter_dimension=0, tiled=True
    )
    position = lengths + step
    query = rope(proj[:, :qcols].reshape(local_rows, groups, per_group, head_dim), position).astype(
        jnp.bfloat16
    )
    kv = proj[:, qcols:].reshape(local_rows, groups, 2 * head_dim)
    new_keys.append(rope(kv[:, :, :head_dim], position).astype(jnp.bfloat16))
    new_vals.append(kv[:, :, head_dim:].astype(jnp.bfloat16))
    keys_now = jnp.stack(new_keys, axis=2)
    vals_now = jnp.stack(new_vals, axis=2)
    scale = 1.0 / head_dim**0.5
    live = (jnp.arange(slots, dtype=jnp.int32)[None, :] < lengths[:, None])[:, None, None, :]
    cached = (
        jnp.einsum("rgjd,rgcd->rgjc", query, key_cache, preferred_element_type=jnp.float32) * scale
    )
    cached = jnp.where(live, cached, -1e30)
    fresh = (
        jnp.einsum("rgjd,rgsd->rgjs", query, keys_now, preferred_element_type=jnp.float32) * scale
    )
    top = jnp.maximum(jnp.max(cached, axis=-1), jnp.max(fresh, axis=-1))
    e_cached = jnp.where(live, jnp.exp(cached - top[..., None]), 0.0)
    e_fresh = jnp.exp(fresh - top[..., None])
    total = jnp.sum(e_cached, axis=-1) + jnp.sum(e_fresh, axis=-1)
    p_cached = (e_cached / total[..., None]).astype(jnp.bfloat16)
    p_fresh = (e_fresh / total[..., None]).astype(jnp.bfloat16)
    out = jnp.einsum("rgjc,rgcd->rgjd", p_cached, value_cache, preferred_element_type=jnp.float32)
    out = out + jnp.einsum("rgjs,rgsd->rgjd", p_fresh, vals_now, preferred_element_type=jnp.float32)
    attended = out.astype(jnp.bfloat16).reshape(local_rows, groups * per_group * head_dim)
    return jnp.dot(
        jnp.concatenate(
            [
                lax.all_gather(attended[:, i * 1024 : (i + 1) * 1024], "wide", axis=0, tiled=True)
                for i in range(attended.shape[1] // 1024)
            ],
            axis=1,
        ),
        w_out,
        preferred_element_type=jnp.float32,
    )


def narrow_gather(state, n_narrow):
    rows, cols = state.shape
    half = rows // 2
    parts = [
        lax.all_gather(state[h * half : (h + 1) * half], "narrow", axis=0, tiled=True).reshape(
            n_narrow, 1, half, cols
        )
        for h in range(2)
    ]
    return jnp.concatenate(parts, axis=1).reshape(n_narrow * rows, cols)


def on_device(hidden_in, w_query, w_keyval, w_out, key_cache, value_cache, lengths):
    w_q2 = w_query.reshape(w_query.shape[0], -1)
    w_kv2 = w_keyval.reshape(w_keyval.shape[0], -1)
    new_keys = []
    new_vals = []
    result = hidden_in
    for step in range(STEPS):
        partial_value = attend_step(
            (
                lax.all_gather(result, "narrow", axis=0, tiled=True)
                if step == 0
                else narrow_gather(result, lax.axis_size("narrow"))
            ),
            step,
            w_q2,
            w_kv2,
            w_out,
            key_cache,
            value_cache,
            lengths,
            new_keys,
            new_vals,
        )
        update = lax.psum_scatter(partial_value, "narrow", scatter_dimension=0, tiled=True)
        result = (result.astype(jnp.float32) + update).astype(jnp.bfloat16)
    return result


def solution(mesh):
    placed = (
        P("narrow", "wide"),
        P("wide", "narrow", None),
        P("wide", "narrow", None),
        P("narrow", "wide"),
        P("wide", "narrow", None, None),
        P("wide", "narrow", None, None),
        P("wide"),
    )
    return jax.shard_map(
        on_device, mesh=mesh, in_specs=placed, out_specs=P("narrow", "wide"), check_vma=False
    )
```

profile of v0, /device:TPU:0, one launch (start us, length us, event | category | flops | bytes accessed | tf_op | source)
XLA Modules:
  0.0 656.7 jit_solution(6499864838221455631)
XLA Ops:
  6.5 0.7 all-gather.2.cloned.1.call-update
  7.3 17.5 %copy.69 = bf16[256,8,2,2048]{3,1,2,0:T(8,128)(2,1)} copy(bf16[256,8,2,2048]{3,2,1,0:T(2,128)(2,1)} %bitcast.62) | data formatting | bytes 33554432
  24.8 0.5 copy.70
  25.3 3.1 all-gather.2.cloned.1.call-done
  28.4 10.5 %fusion.80 = f32[256,4096]{1,0:T(8,128)S(1)} fusion(bf16[256,2048]{1,0:T(8,128)(2,1)} %all-gather.2.cloned.1.call-done, bf16[2048,4096]{1,0:T(8,128)(2,1)} %bitcast.63), kind=kOutput, calls=%fused_computation.122 | convolution fusion | flops 4294967296 | bytes 22020096 | tf_op jit(solution)/shard_map/dot_general | solution.py:33
  38.9 0.7 fusion.81
  39.6 2.5 pad_maximum_fusion
  42.2 0.6 copy-done.4
  42.9 0.2 multiply_cosine_fusion
  43.1 94.6 %reduce-scatter.5.cloned.1.call-done = f32[32,4608]{1,0:T(8,128)} async-done(((f32[256,4608]{1,0:T(8,128)}), f32[32,4608]{1,0:T(8,128)}) %reduce-scatter.5.cloned.1.call-update) | async-done | bytes 589840 | tf_op jit(solution)/shard_map/reduce_scatter | solution.py:35
  137.7 0.8 slice.107
  138.7 1.1 slice_bitcast_fusion.1
  139.9 0.2 subtract_convert_fusion.1
  140.2 0.3 fusion.38
  140.5 12.2 %fusion = (f32[32,2,16]{2,1,0:T(2,128)S(1)}, f32[32,2,16,1024]{3,2,1,0:T(8,128)}) fusion(pred[32,1024]{1,0:T(8,128)(4,1)S(1)} %iota_compare_fusion, bf16[32,2,1024,128]{3,2,1,0:T(8,128)(2,1)} %param.11, bf16[32,2,16,64]{3,2,1,0:T(8,128)(2,1)S(1)} %get-tuple-element.8, bf16[32,2,16,64]{3,2,1,0:T(8,128)(2,1)S(1)} %get-tuple-element.7), kind=kOutput, calls=%fused_computation.8 | convolution fusion | flops 272104448 | bytes 21270528 | tf_op jit(solution)/shard_map/rgjd,rgcd->rgjc/dot_general | solution.py:50
  152.8 3.8 fusion.2
  156.7 7.5 %fusion.35 = bf16[32,2,16,128]{3,2,1,0:T(8,128)(2,1)S(1)} fusion(bf16[32,2,1024,128]{3,2,1,0:T(8,128)(2,1)} %param.12, f32[32,2,16,1024]{3,2,1,0:T(8,128)S(1)} %copy-done.1, f32[32,2,16]{2,1,0:T(2,128)S(1)} %get-tuple-element.22, f32[32,2,16]{2,1,0:T(2,128)S(1)} %multiply_maximum_fusion, pred[32,1024]{1,0:T(8,128)(4,1)S(1)} %iota_compare_fusion, ...), kind=kOutput, calls=%fused_computation.44 | convolution fusion | flops 275120128 | bytes 21311488 | tf_op jit(solution)/shard_map/rgjc,rgcd->rgjd/dot_general | solution.py:62
  164.2 0.1 copy.104
  164.4 31.5 %all_gather.34 = bf16[256,1024]{1,0:T(8,128)(2,1)S(1)} all-gather(bf16[32,1024]{1,0:T(8,128)(2,1)S(1)} %get-tuple-element.15), channel_id=1, replica_groups=mesh['narrow'=4,'wide'=8] {'wide'}, dimensions={0}, use_global_device_ids=true | all-gather | bytes 589824 | tf_op jit(solution)/shard_map/all_gather | solution.py:68
  195.9 31.4 %all_gather.35 = bf16[256,1024]{1,0:T(8,128)(2,1)S(1)} all-gather(bf16[32,1024]{1,0:T(8,128)(2,1)S(1)} %get-tuple-element.18), channel_id=1, replica_groups=mesh['narrow'=4,'wide'=8] {'wide'}, dimensions={0}, use_global_device_ids=true | all-gather | bytes 589824 | tf_op jit(solution)/shard_map/all_gather | solution.py:68
  227.2 31.5 %all_gather.36 = bf16[256,1024]{1,0:T(8,128)(2,1)S(1)} all-gather(bf16[32,1024]{1,0:T(8,128)(2,1)S(1)} %get-tuple-element.17), channel_id=1, replica_groups=mesh['narrow'=4,'wide'=8] {'wide'}, dimensions={0}, use_global_device_ids=true | all-gather | bytes 589824 | tf_op jit(solution)/shard_map/all_gather | solution.py:68
  258.7 31.2 %all_gather.37 = bf16[256,1024]{1,0:T(8,128)(2,1)S(1)} all-gather(bf16[32,1024]{1,0:T(8,128)(2,1)S(1)} %get-tuple-element.16), channel_id=1, replica_groups=mesh['narrow'=4,'wide'=8] {'wide'}, dimensions={0}, use_global_device_ids=true | all-gather | bytes 589824 | tf_op jit(solution)/shard_map/all_gather | solution.py:68
  289.9 10.2 %fusion.6 = f32[256,2048]{1,0:T(8,128)} fusion(bf16[4096,2048]{1,0:T(8,128)(2,1)} %param.10, bf16[256,1024]{1,0:T(8,128)(2,1)S(1)} %all_gather.37, bf16[256,1024]{1,0:T(8,128)(2,1)S(1)} %all_gather.36, bf16[256,1024]{1,0:T(8,128)(2,1)S(1)} %all_gather.35, bf16[256,1024]{1,0:T(8,128)(2,1)S(1)} %all_gather.34), kind=kOutput, calls=%fused_computation.14 | convolution fusion | flops 4303355904 | bytes 20971520 | tf_op jit(solution)/shard_map/dot_general | solution.py:65
  300.2 31.1 %reduce-scatter.7.cloned.1.call-done = f32[64,2048]{1,0:T(8,128)} async-done(((f32[256,2048]{1,0:T(8,128)}), f32[64,2048]{1,0:T(8,128)}) %reduce-scatter.7.cloned.1.call-update) | async-done | bytes 524304 | tf_op jit(solution)/shard_map/reduce_scatter | solution.py:113
  331.3 1.1 add_convert_fusion.2
  332.4 6.8 %all_gather.38 = bf16[128,2048]{1,0:T(8,128)(2,1)S(1)} all-gather(bf16[32,2048]{1,0:T(8,128)(2,1)S(1)} %get-tuple-element.13), channel_id=1, replica_groups=mesh['narrow'=4,'wide'=8] {'narrow'}, dimensions={0}, use_global_device_ids=true | all-gather | bytes 655360 | tf_op jit(solution)/shard_map/all_gather | solution.py:82
  339.2 7.3 %all_gather.39 = bf16[128,2048]{1,0:T(8,128)(2,1)S(1)} all-gather(bf16[32,2048]{1,0:T(8,128)(2,1)S(1)} %get-tuple-element.14), channel_id=1, replica_groups=mesh['narrow'=4,'wide'=8] {'narrow'}, dimensions={0}, use_global_device_ids=true | all-gather | bytes 655360 | tf_op jit(solution)/shard_map/all_gather | solution.py:82
  346.6 8.2 %fusion.82 = f32[256,4096]{1,0:T(8,128)S(1)} fusion(bf16[256,2048]{1,0:T(8,128)(2,1)S(1)} %bitcast.72, bf16[2048,4096]{1,0:T(8,128)(2,1)} %bitcast.64), kind=kOutput, calls=%fused_computation.124 | convolution fusion | flops 4294967296 | bytes 22020096 | tf_op jit(solution)/shard_map/dot_general | solution.py:33
  354.7 0.7 fusion.83
  355.5 2.5 pad_maximum_fusion.1
  358.2 95.8 %reduce-scatter.9.cloned.1.call-done = f32[32,4608]{1,0:T(8,128)} async-done(((f32[256,4608]{1,0:T(8,128)}), f32[32,4608]{1,0:T(8,128)}) %reduce-scatter.9.cloned.1.call-update) | async-done | bytes 589840 | tf_op jit(solution)/shard_map/reduce_scatter | solution.py:35
  454.0 0.8 slice.120
  455.1 1.1 slice_bitcast_fusion
  456.3 0.2 subtract_convert_fusion
  456.5 12.2 %fusion.1 = (f32[32,2,16]{2,1,0:T(2,128)S(1)}, f32[32,2,16,1024]{3,2,1,0:T(8,128)}) fusion(pred[32,1024]{1,0:T(8,128)(4,1)S(1)} %iota_compare_fusion, bf16[32,2,1024,128]{3,2,1,0:T(8,128)(2,1)} %param.11, bf16[32,2,16,64]{3,2,1,0:T(8,128)(2,1)S(1)} %get-tuple-element.6, bf16[32,2,16,64]{3,2,1,0:T(8,128)(2,1)S(1)} %get-tuple-element.5), kind=kOutput, calls=%fused_computation.9 | convolution fusion | flops 272104448 | bytes 21270528 | tf_op jit(solution)/shard_map/rgjd,rgcd->rgjc/dot_general | solution.py:50
  468.7 0.5 fusion.79
  469.3 0.1 fusion.40
  469.4 3.9 fusion.3
  473.4 7.3 %fusion.5 = f32[32,2,16,128]{3,2,1,0:T(8,128)S(1)} fusion(bf16[32,2,1024,128]{3,2,1,0:T(8,128)(2,1)} %param.12, f32[32,2,16,1024]{3,2,1,0:T(8,128)S(1)} %copy-done, f32[32,2,16]{2,1,0:T(2,128)S(1)} %add.59, f32[32,2,16]{2,1,0:T(2,128)S(1)} %max.13, pred[32,1024]{1,0:T(8,128)(4,1)S(1)} %iota_compare_fusion), kind=kOutput, calls=%fused_computation.13 | convolution fusion | flops 274726912 | bytes 21536768 | tf_op jit(solution)/shard_map/rgjc,rgcd->rgjd/dot_general | solution.py:62
  480.8 0.3 fusion.36
  481.1 0.1 copy.103
  481.2 31.5 %all_gather.40 = bf16[256,1024]{1,0:T(8,128)(2,1)S(1)} all-gather(bf16[32,1024]{1,0:T(8,128)(2,1)S(1)} %get-tuple-element.9), channel_id=1, replica_groups=mesh['narrow'=4,'wide'=8] {'wide'}, dimensions={0}, use_global_device_ids=true | all-gather | bytes 589824 | tf_op jit(solution)/shard_map/all_gather | solution.py:68
  512.7 31.3 %all_gather.41 = bf16[256,1024]{1,0:T(8,128)(2,1)S(1)} all-gather(bf16[32,1024]{1,0:T(8,128)(2,1)S(1)} %get-tuple-element.12), channel_id=1, replica_groups=mesh['narrow'=4,'wide'=8] {'wide'}, dimensions={0}, use_global_device_ids=true | all-gather | bytes 589824 | tf_op jit(solution)/shard_map/all_gather | solution.py:68
  544.1 31.6 %all_gather.42 = bf16[256,1024]{1,0:T(8,128)(2,1)S(1)} all-gather(bf16[32,1024]{1,0:T(8,128)(2,1)S(1)} %get-tuple-element.11), channel_id=1, replica_groups=mesh['narrow'=4,'wide'=8] {'wide'}, dimensions={0}, use_global_device_ids=true | all-gather | bytes 589824 | tf_op jit(solution)/shard_map/all_gather | solution.py:68
  575.7 31.2 %all_gather.43 = bf16[256,1024]{1,0:T(8,128)(2,1)S(1)} all-gather(bf16[32,1024]{1,0:T(8,128)(2,1)S(1)} %get-tuple-element.10), channel_id=1, replica_groups=mesh['narrow'=4,'wide'=8] {'wide'}, dimensions={0}, use_global_device_ids=true | all-gather | bytes 589824 | tf_op jit(solution)/shard_map/all_gather | solution.py:68
  606.8 10.2 %fusion.14 = f32[256,2048]{1,0:T(8,128)} fusion(bf16[4096,2048]{1,0:T(8,128)(2,1)} %param.10, bf16[256,1024]{1,0:T(8,128)(2,1)S(1)} %all_gather.43, bf16[256,1024]{1,0:T(8,128)(2,1)S(1)} %all_gather.42, bf16[256,1024]{1,0:T(8,128)(2,1)S(1)} %all_gather.41, bf16[256,1024]{1,0:T(8,128)(2,1)S(1)} %all_gather.40), kind=kOutput, calls=%fused_computation.22 | convolution fusion | flops 4303355904 | bytes 20971520 | tf_op jit(solution)/shard_map/dot_general | solution.py:65
  617.0 31.4 %reduce-scatter.11.cloned.1.call-done = f32[64,2048]{1,0:T(8,128)} async-done(((f32[256,2048]{1,0:T(8,128)}), f32[64,2048]{1,0:T(8,128)}) %reduce-scatter.11.cloned.1.call-update) | async-done | bytes 524304 | tf_op jit(solution)/shard_map/reduce_scatter | solution.py:113
  648.4 1.8 add_convert_fusion
  (51 shorter events, 1.4 us)
Async XLA Ops:
  6.5 21.8 %all-gather.2.cloned.1.call-start = ((), (), s32[]{:S(2)}) async-start(), calls=%async_computation.4 | async-start | bytes 1310720 | tf_op jit(solution)/shard_map/all_gather | solution.py:99
  7.3 130.4 %reduce-scatter.5.cloned.1.call-start = ((), (), s32[]{:S(2)}) async-start(), calls=%async_computation.5 | async-start | bytes 5308416 | tf_op jit(solution)/shard_map/reduce_scatter | solution.py:35
  7.3 17.5 %copy-start.2 = (bf16[2048,2,256]{2,1,0:T(2,128)(2,1)S(1)}, bf16[2048,2,256]{2,1,0:T(2,128)(2,1)}, u32[]{:S(2)}) copy-start(bf16[2048,2,256]{2,1,0:T(2,128)(2,1)} %param.9) | copy-start | bytes 6291460
  28.4 10.5 %copy-start.5 = (bf16[256,2048]{1,0:T(8,128)(2,1)S(1)}, bf16[256,2048]{1,0:T(8,128)(2,1)}, u32[]{:S(2)}) copy-start(bf16[256,2048]{1,0:T(8,128)(2,1)} %all-gather.2.cloned.1.call-done) | copy-start | bytes 3145732
  42.1 0.7 copy-start.4
  42.2 289.1 %reduce-scatter.7.cloned.1.call-start = ((), (), s32[]{:S(2)}) async-start(), calls=%async_computation.6 | async-start | bytes 2621440 | tf_op jit(solution)/shard_map/reduce_scatter | solution.py:113
  152.8 3.9 copy-start.1
  289.9 41.4 %copy-start.3 = (bf16[64,2048]{1,0:T(8,128)(2,1)S(1)}, bf16[64,2048]{1,0:T(8,128)(2,1)}, u32[]{:S(2)}) copy-start(bf16[64,2048]{1,0:T(8,128)(2,1)} %param.7) | copy-start | bytes 786436
  300.1 153.8 %reduce-scatter.9.cloned.1.call-start = ((), (), s32[]{:S(2)}) async-start(), calls=%async_computation.7 | async-start | bytes 5308416 | tf_op jit(solution)/shard_map/reduce_scatter | solution.py:35
  358.0 290.4 %reduce-scatter.11.cloned.1.call-start = ((), (), s32[]{:S(2)}) async-start(), calls=%async_computation.8 | async-start | bytes 2621440 | tf_op jit(solution)/shard_map/reduce_scatter | solution.py:113
  468.7 4.7 copy-start
Sparse Core Ops, SparseCore 0:
  8.9 19.4 all-gather.1
  42.3 95.3 reduce-scatter.4
  300.3 30.9 reduce-scatter.6
  358.1 95.7 reduce-scatter.8
  617.2 31.1 reduce-scatter.10
where the time goes:
time: 657 us
  blocking collectives  265 us (40%)
  waiting for transfers between devices  257 us (39%)
  matrix products  80.9 us (12%)
  local copies, waits for them, and re-layouts  23.4 us (4%)
  other arithmetic  16.9 us (3%)
  between operations  13.5 us (2%)
    all_gather x8, blocking collectives, attend_step(): lax.all_gather(attended[:, i * 1024:(i + 1) * 1024], 'wide', axis=0, tile...  251 us
    reduce_scatter x2, waiting for transfers between devices, attend_step(): lax.psum_scatter(jnp.concatenate((part_q, part_kv), axis=1), 'wide', scat...  190 us
    reduce_scatter x2, waiting for transfers between devices, on_device(): lax.psum_scatter(partial_value, 'narrow', scatter_dimension=0, tiled=True)  62.4 us
    dot_general x2, matrix products, attend_step(): jnp.einsum('rgjd,rgcd->rgjc', query, key_cache, preferred_element_type=jn...  24.5 us
    unnamed x21, local copies, waits for them, and re-layouts  21.2 us
    dot_general x2, matrix products, attend_step(): jnp.dot(jnp.concatenate([lax.all_gather(attended[:, i * 1024:(i + 1) * 10...  20.4 us
    dot_general x2, matrix products, attend_step(): part_q = jnp.dot(every, w_q2, preferred_element_type=jnp.float32)  18.6 us
    dot_general x2, matrix products, attend_step(): jnp.einsum('rgjc,rgcd->rgjd', p_cached, value_cache, preferred_element_ty...  14.8 us
  transfers between devices with their start and end apart: 5, of which 5 were waited for; matrix products, arithmetic and copies ran while one was open for 3% of the time, Pallas kernels for 0%

commit v1 on v0

--- a/solution.py
+++ b/solution.py
@@ -5,6 +5,18 @@
 
 STEPS = 2
 rope_base = 500000.0
+
+
+def collect(array, axis, dim):
+    ways, here, step = (lax.axis_size(axis), lax.axis_index(axis), array.shape[dim])
+    line, have = (array, 1)
+    while have < ways:
+        line = jnp.concatenate(
+            [line, lax.ppermute(line, axis, [(d, (d - have) % ways) for d in range(ways)])],
+            axis=dim,
+        )
+        have = 2 * have
+    return jnp.roll(line, here * step, axis=dim)
 
 
 def rope(values, position):
@@ -65,7 +77,7 @@
     return jnp.dot(
         jnp.concatenate(
             [
-                lax.all_gather(attended[:, i * 1024 : (i + 1) * 1024], "wide", axis=0, tiled=True)
+                collect(attended[:, i * 1024 : (i + 1) * 1024], "wide", 0)
                 for i in range(attended.shape[1] // 1024)
             ],
             axis=1,

time: 657 us -> 552 us (0.84); the launches traced: 657 us -> 543 us
  blocking collectives: 265 us -> 14.2 us
  waiting for transfers between devices: 257 us -> 325 us
  starting transfers between devices: 0.17 us -> 54 us
  other arithmetic: 16.9 us -> 31.8 us
    all_gather x8 -> x0, blocking collectives: 251 us -> none  [attend_step(): lax.all_gather(attended[:, i * 1024:(i + 1) * 1024], 'wide', axis=0, tile...]
    ppermute x0 -> x24, waiting for transfers between devices: none -> 67.1 us  [collect(): lax.ppermute(line, axis, [(d, (d - have) % ways) for d in range(ways)])]
    ppermute x0 -> x24, starting transfers between devices: none -> 53.8 us  [collect(): lax.ppermute(line, axis, [(d, (d - have) % ways) for d in range(ways)])]
    concatenate x0 -> x24, other arithmetic: none -> 14.9 us  [the longest x8 14.6 us: collect(): return jnp.roll(line, here * step, axis=dim)]
  transfers between devices with their start and end apart: 5 -> 29, of which waited for: 5 -> 21; matrix products, arithmetic and copies ran while one was open for 3% -> 5% of each run, Pallas kernels for 0% -> 0%
where the time goes in v1:
time: 552 us; the launch traced here: 543 us
  waiting for transfers between devices  325 us (59%)
  matrix products  81 us (15%)
  starting transfers between devices  54 us (10%)
  other arithmetic  31.8 us (6%)
  local copies, waits for them, and re-layouts  23.4 us (4%)
  blocking collectives  14.2 us (3%)
  between operations  13.9 us (3%)
    reduce_scatter x2, waiting for transfers between devices, attend_step(): lax.psum_scatter(jnp.concatenate((part_q, part_kv), axis=1), 'wide', scat...  190 us
    ppermute x24, waiting for transfers between devices, collect(): lax.ppermute(line, axis, [(d, (d - have) % ways) for d in range(ways)])  67.1 us
    reduce_scatter x2, waiting for transfers between devices, on_device(): lax.psum_scatter(partial_value, 'narrow', scatter_dimension=0, tiled=True)  63.8 us
    ppermute x24, starting transfers between devices, collect(): lax.ppermute(line, axis, [(d, (d - have) % ways) for d in range(ways)])  53.8 us
    dot_general x2, matrix products, attend_step(): jnp.einsum('rgjd,rgcd->rgjc', query, key_cache, preferred_element_type=jn...  24.5 us
    unnamed x21, local copies, waits for them, and re-layouts  21.2 us
    dot_general x2, matrix products, attend_step(): jnp.dot(jnp.concatenate([collect(attended[:, i * 1024:(i + 1) * 1024], 'w...  20.4 us
    dot_general x2, matrix products, attend_step(): part_q = jnp.dot(every, w_q2, preferred_element_type=jnp.float32)  18.7 us
  transfers between devices with their start and end apart: 29, of which 21 were waited for; matrix products, arithmetic and copies ran while one was open for 5% of the time, Pallas kernels for 0%

profile of v1, /device:TPU:0, one launch (start us, length us, event | category | flops | bytes accessed | tf_op | source)
XLA Modules:
  0.0 543.4 jit_solution(9354478611500911644)
XLA Ops:
  7.3 17.5 %copy.69 = bf16[256,8,2,2048]{3,1,2,0:T(8,128)(2,1)} copy(bf16[256,8,2,2048]{3,2,1,0:T(2,128)(2,1)} %bitcast.62) | data formatting | bytes 33554432
  25.3 3.0 all-gather.2.cloned.1.call-done
  28.4 10.5 %fusion.136 = f32[256,4096]{1,0:T(8,128)S(1)} fusion(bf16[256,2048]{1,0:T(8,128)(2,1)} %all-gather.2.cloned.1.call-done, bf16[2048,4096]{1,0:T(8,128)(2,1)} %bitcast.63), kind=kOutput, calls=%fused_computation.258 | convolution fusion | flops 4294967296 | bytes 22020096 | tf_op jit(solution)/shard_map/dot_general | solution.py:45
  39.7 2.6 pad_maximum_fusion
  43.2 94.6 %reduce-scatter.5.cloned.1.call-done = f32[32,4608]{1,0:T(8,128)} async-done(((f32[256,4608]{1,0:T(8,128)}), f32[32,4608]{1,0:T(8,128)}) %reduce-scatter.5.cloned.1.call-update) | async-done | bytes 589840 | tf_op jit(solution)/shard_map/reduce_scatter | solution.py:47
  140.7 12.3 %fusion = (f32[32,2,16]{2,1,0:T(2,128)S(1)}, f32[32,2,16,1024]{3,2,1,0:T(8,128)}) fusion(pred[32,1024]{1,0:T(8,128)(4,1)S(1)} %iota_compare_fusion, bf16[32,2,1024,128]{3,2,1,0:T(8,128)(2,1)} %param.13, bf16[32,2,16,64]{3,2,1,0:T(8,128)(2,1)S(1)} %get-tuple-element.9, bf16[32,2,16,64]{3,2,1,0:T(8,128)(2,1)S(1)} %get-tuple-element.8), kind=kOutput, calls=%fused_computation.8 | convolution fusion | flops 272104448 | bytes 21270528 | tf_op jit(solution)/shard_map/rgjd,rgcd->rgjc/dot_general | solution.py:62
  153.0 3.8 fusion.2
  156.9 7.5 %fusion.35 = bf16[32,2,16,128]{3,2,1,0:T(8,128)(2,1)S(1)} fusion(bf16[32,2,1024,128]{3,2,1,0:T(8,128)(2,1)} %param.14, f32[32,2,16,1024]{3,2,1,0:T(8,128)S(1)} %copy-done.1, f32[32,2,16]{2,1,0:T(2,128)S(1)} %get-tuple-element.23, f32[32,2,16]{2,1,0:T(2,128)S(1)} %multiply_maximum_fusion, pred[32,1024]{1,0:T(8,128)(4,1)S(1)} %iota_compare_fusion, ...), kind=kOutput, calls=%fused_computation.44 | convolution fusion | flops 275120128 | bytes 21311488 | tf_op jit(solution)/shard_map/rgjc,rgcd->rgjd/dot_general | solution.py:74
  164.5 3.1 collective-permute-start
  168.7 2.4 collective-permute-start.6
  172.6 1.9 collective-permute-start.4
  176.9 1.9 collective-permute-done.1
  179.8 1.8 collective-permute-done.4
  186.3 1.9 collective-permute-start.11
  188.3 26.6 %collective-permute-done.2 = bf16[128,1024]{1,0:T(8,128)(2,1)S(1)} collective-permute-done((bf16[128,1024]{1,0:T(8,128)(2,1)S(1)}, bf16[128,1024]{1,0:T(8,128)(2,1)S(1)}, u32[]{:S(2)}, u32[]{:S(2)}) %collective-permute-start.2) | collective-permute-done | bytes 262176 | tf_op jit(solution)/shard_map/ppermute | solution.py:15
  214.8 1.8 fusion.89
  216.6 3.8 collective-permute-done.5
  220.4 1.8 fusion.82
  222.3 3.8 collective-permute-done.8
  226.0 1.8 fusion.75
  227.9 2.8 collective-permute-done.11
  230.6 1.8 fusion.68
  232.5 10.2 %fusion.6 = f32[256,2048]{1,0:T(8,128)} fusion(bf16[4096,2048]{1,0:T(8,128)(2,1)} %param.12, bf16[256,1024]{1,0:T(8,128)(2,1)S(1)} %fusion.68, bf16[256,1024]{1,0:T(8,128)(2,1)S(1)} %fusion.75, bf16[256,1024]{1,0:T(8,128)(2,1)S(1)} %fusion.82, bf16[256,1024]{1,0:T(8,128)(2,1)S(1)} %fusion.89), kind=kOutput, calls=%fused_computation.14 | convolution fusion | flops 4303355904 | bytes 20971520 | tf_op jit(solution)/shard_map/dot_general | solution.py:77
  242.8 31.9 %reduce-scatter.7.cloned.1.call-done = f32[64,2048]{1,0:T(8,128)} async-done(((f32[256,2048]{1,0:T(8,128)}), f32[64,2048]{1,0:T(8,128)}) %reduce-scatter.7.cloned.1.call-update) | async-done | bytes 524304 | tf_op jit(solution)/shard_map/reduce_scatter | solution.py:125
  275.8 6.8 %all_gather.10 = bf16[128,2048]{1,0:T(8,128)(2,1)S(1)} all-gather(bf16[32,2048]{1,0:T(8,128)(2,1)S(1)} %get-tuple-element.14), channel_id=1, replica_groups=mesh['narrow'=4,'wide'=8] {'narrow'}, dimensions={0}, use_global_device_ids=true | all-gather | bytes 655360 | tf_op jit(solution)/shard_map/all_gather | solution.py:94
  282.6 7.4 %all_gather.11 = bf16[128,2048]{1,0:T(8,128)(2,1)S(1)} all-gather(bf16[32,2048]{1,0:T(8,128)(2,1)S(1)} %get-tuple-element.15), channel_id=1, replica_groups=mesh['narrow'=4,'wide'=8] {'narrow'}, dimensions={0}, use_global_device_ids=true | all-gather | bytes 655360 | tf_op jit(solution)/shard_map/all_gather | solution.py:94
  290.2 8.2 %fusion.138 = f32[256,4096]{1,0:T(8,128)S(1)} fusion(bf16[256,2048]{1,0:T(8,128)(2,1)S(1)} %bitcast.72, bf16[2048,4096]{1,0:T(8,128)(2,1)} %bitcast.64), kind=kOutput, calls=%fused_computation.260 | convolution fusion | flops 4294967296 | bytes 22020096 | tf_op jit(solution)/shard_map/dot_general | solution.py:45
  299.1 2.6 pad_maximum_fusion.1
  301.8 95.8 %reduce-scatter.9.cloned.1.call-done = f32[32,4608]{1,0:T(8,128)} async-done(((f32[256,4608]{1,0:T(8,128)}), f32[32,4608]{1,0:T(8,128)}) %reduce-scatter.9.cloned.1.call-update) | async-done | bytes 589840 | tf_op jit(solution)/shard_map/reduce_scatter | solution.py:47
  400.1 12.3 %fusion.1 = (f32[32,2,16]{2,1,0:T(2,128)S(1)}, f32[32,2,16,1024]{3,2,1,0:T(8,128)}) fusion(pred[32,1024]{1,0:T(8,128)(4,1)S(1)} %iota_compare_fusion, bf16[32,2,1024,128]{3,2,1,0:T(8,128)(2,1)} %param.13, bf16[32,2,16,64]{3,2,1,0:T(8,128)(2,1)S(1)} %get-tuple-element.7, bf16[32,2,16,64]{3,2,1,0:T(8,128)(2,1)S(1)} %get-tuple-element.6), kind=kOutput, calls=%fused_computation.9 | convolution fusion | flops 272104448 | bytes 21270528 | tf_op jit(solution)/shard_map/rgjd,rgcd->rgjc/dot_general | solution.py:62
  413.1 3.9 fusion.3
  417.1 7.3 %fusion.5 = f32[32,2,16,128]{3,2,1,0:T(8,128)S(1)} fusion(bf16[32,2,1024,128]{3,2,1,0:T(8,128)(2,1)} %param.14, f32[32,2,16,1024]{3,2,1,0:T(8,128)S(1)} %copy-done, f32[32,2,16]{2,1,0:T(2,128)S(1)} %add.67, f32[32,2,16]{2,1,0:T(2,128)S(1)} %max.13, pred[32,1024]{1,0:T(8,128)(4,1)S(1)} %iota_compare_fusion), kind=kOutput, calls=%fused_computation.13 | convolution fusion | flops 274726912 | bytes 21536768 | tf_op jit(solution)/shard_map/rgjc,rgcd->rgjd/dot_general | solution.py:74
  424.9 3.1 collective-permute-start.12
  428.6 2.4 collective-permute-start.18
  432.5 1.9 collective-permute-start.16
  436.9 1.8 collective-permute-done.13
  446.3 20.2 %collective-permute-start.23 = (bf16[128,1024]{1,0:T(8,128)(2,1)S(1)}, bf16[128,1024]{1,0:T(8,128)(2,1)S(1)}, u32[]{:S(2)}, u32[]{:S(2)}) collective-permute-start(bf16[128,1024]{1,0:T(8,128)(2,1)S(1)} %pad_maximum_fusion.12), channel_id=1, source_target_pairs={{0,4},{1,5},{2,6},{3,7},{4,0},{5,1},{6,2},{7,3},{8,12},{9,13},{10,... | collective-permute-start | bytes 786440 | tf_op jit(solution)/shard_map/ppermute | solution.py:15
  466.5 8.9 %collective-permute-done.14 = bf16[128,1024]{1,0:T(8,128)(2,1)S(1)} collective-permute-done((bf16[128,1024]{1,0:T(8,128)(2,1)S(1)}, bf16[128,1024]{1,0:T(8,128)(2,1)S(1)}, u32[]{:S(2)}, u32[]{:S(2)}) %collective-permute-start.14) | collective-permute-done | bytes 262176 | tf_op jit(solution)/shard_map/ppermute | solution.py:15
  475.4 1.8 fusion.61
  477.2 3.8 collective-permute-done.17
  481.0 1.8 fusion.54
  482.9 3.8 collective-permute-done.20
  486.7 1.8 fusion.47
  488.5 2.5 collective-permute-done.23
  490.9 1.8 fusion.40
  492.8 10.2 %fusion.14 = f32[256,2048]{1,0:T(8,128)} fusion(bf16[4096,2048]{1,0:T(8,128)(2,1)} %param.12, bf16[256,1024]{1,0:T(8,128)(2,1)S(1)} %fusion.40, bf16[256,1024]{1,0:T(8,128)(2,1)S(1)} %fusion.47, bf16[256,1024]{1,0:T(8,128)(2,1)S(1)} %fusion.54, bf16[256,1024]{1,0:T(8,128)(2,1)S(1)} %fusion.61), kind=kOutput, calls=%fused_computation.22 | convolution fusion | flops 4303355904 | bytes 20971520 | tf_op jit(solution)/shard_map/dot_general | solution.py:77
  503.0 31.9 %reduce-scatter.11.cloned.1.call-done = f32[64,2048]{1,0:T(8,128)} async-done(((f32[256,2048]{1,0:T(8,128)}), f32[64,2048]{1,0:T(8,128)}) %reduce-scatter.11.cloned.1.call-update) | async-done | bytes 524304 | tf_op jit(solution)/shard_map/reduce_scatter | solution.py:125
  534.9 1.8 add_convert_fusion
  (115 shorter events, 34.6 us)
Async XLA Ops:
  6.5 21.8 %all-gather.2.cloned.1.call-start = ((), (), s32[]{:S(2)}) async-start(), calls=%async_computation.4 | async-start | bytes 1310720 | tf_op jit(solution)/shard_map/all_gather | solution.py:111
  7.3 130.6 %reduce-scatter.5.cloned.1.call-start = ((), (), s32[]{:S(2)}) async-start(), calls=%async_computation.5 | async-start | bytes 5308416 | tf_op jit(solution)/shard_map/reduce_scatter | solution.py:47
  7.3 17.5 %copy-start.2 = (bf16[2048,2,256]{2,1,0:T(2,128)(2,1)S(1)}, bf16[2048,2,256]{2,1,0:T(2,128)(2,1)}, u32[]{:S(2)}) copy-start(bf16[2048,2,256]{2,1,0:T(2,128)(2,1)} %param.11) | copy-start | bytes 6291460
  28.4 10.6 %copy-start.5 = (bf16[256,2048]{1,0:T(8,128)(2,1)S(1)}, bf16[256,2048]{1,0:T(8,128)(2,1)}, u32[]{:S(2)}) copy-start(bf16[256,2048]{1,0:T(8,128)(2,1)} %all-gather.2.cloned.1.call-done) | copy-start | bytes 3145732
  42.2 0.7 copy-start.4
  42.3 232.4 %reduce-scatter.7.cloned.1.call-start = ((), (), s32[]{:S(2)}) async-start(), calls=%async_computation.6 | async-start | bytes 2621440 | tf_op jit(solution)/shard_map/reduce_scatter | solution.py:125
  152.9 3.9 copy-start.1
  164.5 7.1 %collective-permute-start = (bf16[32,1024]{1,0:T(8,128)(2,1)S(1)}, bf16[32,1024]{1,0:T(8,128)(2,1)S(1)}, u32[]{:S(2)}, u32[]{:S(2)}) collective-permute-start(bf16[32,1024]{1,0:T(8,128)(2,1)S(1)} %get-tuple-element.16), channel_id=1, source_target_pairs={{0,7},{1,0},{2,1},{3,2},{4,3},{5,4},{6,5},{7,6},{8,15},{9,8},{10,9... | collective-permute-start | bytes 196616 | tf_op jit(solution)/shard_map/ppermute | solution.py:15
  167.6 4.9 collective-permute-start.3
  168.7 5.8 %collective-permute-start.6 = (bf16[32,1024]{1,0:T(8,128)(2,1)S(1)}, bf16[32,1024]{1,0:T(8,128)(2,1)S(1)}, u32[]{:S(2)}, u32[]{:S(2)}) collective-permute-start(bf16[32,1024]{1,0:T(8,128)(2,1)S(1)} %get-tuple-element.18), channel_id=1, source_target_pairs={{0,7},{1,0},{2,1},{3,2},{4,3},{5,4},{6,5},{7,6},{8,15},{9,8},{10,9... | collective-permute-start | bytes 196616 | tf_op jit(solution)/shard_map/ppermute | solution.py:15
  171.1 4.4 collective-permute-start.9
  171.7 7.1 %collective-permute-start.1 = (bf16[64,1024]{1,0:T(8,128)(2,1)S(1)}, bf16[64,1024]{1,0:T(8,128)(2,1)S(1)}, u32[]{:S(2)}, u32[]{:S(2)}) collective-permute-start(bf16[64,1024]{1,0:T(8,128)(2,1)S(1)} %pad_maximum_fusion.13), channel_id=1, source_target_pairs={{0,6},{1,7},{2,0},{3,1},{4,2},{5,3},{6,4},{7,5},{8,14},{9,15},{10,... | collective-permute-start | bytes 393224 | tf_op jit(solution)/shard_map/ppermute | solution.py:15
  172.6 9.0 %collective-permute-start.4 = (bf16[64,1024]{1,0:T(8,128)(2,1)S(1)}, bf16[64,1024]{1,0:T(8,128)(2,1)S(1)}, u32[]{:S(2)}, u32[]{:S(2)}) collective-permute-start(bf16[64,1024]{1,0:T(8,128)(2,1)S(1)} %pad_maximum_fusion.14), channel_id=1, source_target_pairs={{0,6},{1,7},{2,0},{3,1},{4,2},{5,3},{6,4},{7,5},{8,14},{9,15},{10,... | collective-permute-start | bytes 393224 | tf_op jit(solution)/shard_map/ppermute | solution.py:15
  174.5 9.8 %collective-permute-start.7 = (bf16[64,1024]{1,0:T(8,128)(2,1)S(1)}, bf16[64,1024]{1,0:T(8,128)(2,1)S(1)}, u32[]{:S(2)}, u32[]{:S(2)}) collective-permute-start(bf16[64,1024]{1,0:T(8,128)(2,1)S(1)} %pad_maximum_fusion.15), channel_id=1, source_target_pairs={{0,6},{1,7},{2,0},{3,1},{4,2},{5,3},{6,4},{7,5},{8,14},{9,15},{10,... | collective-permute-start | bytes 393224 | tf_op jit(solution)/shard_map/ppermute | solution.py:15
  175.5 10.8 %collective-permute-start.10 = (bf16[64,1024]{1,0:T(8,128)(2,1)S(1)}, bf16[64,1024]{1,0:T(8,128)(2,1)S(1)}, u32[]{:S(2)}, u32[]{:S(2)}) collective-permute-start(bf16[64,1024]{1,0:T(8,128)(2,1)S(1)} %pad_maximum_fusion.16), channel_id=1, source_target_pairs={{0,6},{1,7},{2,0},{3,1},{4,2},{5,3},{6,4},{7,5},{8,14},{9,15},{10,... | collective-permute-start | bytes 393224 | tf_op jit(solution)/shard_map/ppermute | solution.py:15
  178.8 36.0 %collective-permute-start.2 = (bf16[128,1024]{1,0:T(8,128)(2,1)S(1)}, bf16[128,1024]{1,0:T(8,128)(2,1)S(1)}, u32[]{:S(2)}, u32[]{:S(2)}) collective-permute-start(bf16[128,1024]{1,0:T(8,128)(2,1)S(1)} %pad_maximum_fusion.4), channel_id=1, source_target_pairs={{0,4},{1,5},{2,6},{3,7},{4,0},{5,1},{6,2},{7,3},{8,12},{9,13},{10,... | collective-permute-start | bytes 786440 | tf_op jit(solution)/shard_map/ppermute | solution.py:15
  181.6 38.8 %collective-permute-start.5 = (bf16[128,1024]{1,0:T(8,128)(2,1)S(1)}, bf16[128,1024]{1,0:T(8,128)(2,1)S(1)}, u32[]{:S(2)}, u32[]{:S(2)}) collective-permute-start(bf16[128,1024]{1,0:T(8,128)(2,1)S(1)} %pad_maximum_fusion.5), channel_id=1, source_target_pairs={{0,4},{1,5},{2,6},{3,7},{4,0},{5,1},{6,2},{7,3},{8,12},{9,13},{10,... | collective-permute-start | bytes 786440 | tf_op jit(solution)/shard_map/ppermute | solution.py:15
  184.3 41.7 %collective-permute-start.8 = (bf16[128,1024]{1,0:T(8,128)(2,1)S(1)}, bf16[128,1024]{1,0:T(8,128)(2,1)S(1)}, u32[]{:S(2)}, u32[]{:S(2)}) collective-permute-start(bf16[128,1024]{1,0:T(8,128)(2,1)S(1)} %pad_maximum_fusion.6), channel_id=1, source_target_pairs={{0,4},{1,5},{2,6},{3,7},{4,0},{5,1},{6,2},{7,3},{8,12},{9,13},{10,... | collective-permute-start | bytes 786440 | tf_op jit(solution)/shard_map/ppermute | solution.py:15
  186.3 44.3 %collective-permute-start.11 = (bf16[128,1024]{1,0:T(8,128)(2,1)S(1)}, bf16[128,1024]{1,0:T(8,128)(2,1)S(1)}, u32[]{:S(2)}, u32[]{:S(2)}) collective-permute-start(bf16[128,1024]{1,0:T(8,128)(2,1)S(1)} %pad_maximum_fusion.7), channel_id=1, source_target_pairs={{0,4},{1,5},{2,6},{3,7},{4,0},{5,1},{6,2},{7,3},{8,12},{9,13},{10,... | collective-permute-start | bytes 786440 | tf_op jit(solution)/shard_map/ppermute | solution.py:15
  232.5 42.2 %copy-start.3 = (bf16[64,2048]{1,0:T(8,128)(2,1)S(1)}, bf16[64,2048]{1,0:T(8,128)(2,1)}, u32[]{:S(2)}) copy-start(bf16[64,2048]{1,0:T(8,128)(2,1)} %param.9) | copy-start | bytes 786436
  242.7 154.9 %reduce-scatter.9.cloned.1.call-start = ((), (), s32[]{:S(2)}) async-start(), calls=%async_computation.7 | async-start | bytes 5308416 | tf_op jit(solution)/shard_map/reduce_scatter | solution.py:47
  301.6 233.3 %reduce-scatter.11.cloned.1.call-start = ((), (), s32[]{:S(2)}) async-start(), calls=%async_computation.8 | async-start | bytes 2621440 | tf_op jit(solution)/shard_map/reduce_scatter | solution.py:125
  412.4 4.7 copy-start
  424.9 6.6 %collective-permute-start.12 = (bf16[32,1024]{1,0:T(8,128)(2,1)S(1)}, bf16[32,1024]{1,0:T(8,128)(2,1)S(1)}, u32[]{:S(2)}, u32[]{:S(2)}) collective-permute-start(bf16[32,1024]{1,0:T(8,128)(2,1)S(1)} %get-tuple-element.10), channel_id=1, source_target_pairs={{0,7},{1,0},{2,1},{3,2},{4,3},{5,4},{6,5},{7,6},{8,15},{9,8},{10,9... | collective-permute-start | bytes 196616 | tf_op jit(solution)/shard_map/ppermute | solution.py:15
  428.0 4.5 collective-permute-start.15
  428.6 5.8 %collective-permute-start.18 = (bf16[32,1024]{1,0:T(8,128)(2,1)S(1)}, bf16[32,1024]{1,0:T(8,128)(2,1)S(1)}, u32[]{:S(2)}, u32[]{:S(2)}) collective-permute-start(bf16[32,1024]{1,0:T(8,128)(2,1)S(1)} %get-tuple-element.12), channel_id=1, source_target_pairs={{0,7},{1,0},{2,1},{3,2},{4,3},{5,4},{6,5},{7,6},{8,15},{9,8},{10,9... | collective-permute-start | bytes 196616 | tf_op jit(solution)/shard_map/ppermute | solution.py:15
  430.9 4.6 collective-permute-start.21
  431.5 7.2 %collective-permute-start.13 = (bf16[64,1024]{1,0:T(8,128)(2,1)S(1)}, bf16[64,1024]{1,0:T(8,128)(2,1)S(1)}, u32[]{:S(2)}, u32[]{:S(2)}) collective-permute-start(bf16[64,1024]{1,0:T(8,128)(2,1)S(1)} %pad_maximum_fusion.17), channel_id=1, source_target_pairs={{0,6},{1,7},{2,0},{3,1},{4,2},{5,3},{6,4},{7,5},{8,14},{9,15},{10,... | collective-permute-start | bytes 393224 | tf_op jit(solution)/shard_map/ppermute | solution.py:15
  432.5 9.0 %collective-permute-start.16 = (bf16[64,1024]{1,0:T(8,128)(2,1)S(1)}, bf16[64,1024]{1,0:T(8,128)(2,1)S(1)}, u32[]{:S(2)}, u32[]{:S(2)}) collective-permute-start(bf16[64,1024]{1,0:T(8,128)(2,1)S(1)} %pad_maximum_fusion.18), channel_id=1, source_target_pairs={{0,6},{1,7},{2,0},{3,1},{4,2},{5,3},{6,4},{7,5},{8,14},{9,15},{10,... | collective-permute-start | bytes 393224 | tf_op jit(solution)/shard_map/ppermute | solution.py:15
  434.4 9.8 %collective-permute-start.19 = (bf16[64,1024]{1,0:T(8,128)(2,1)S(1)}, bf16[64,1024]{1,0:T(8,128)(2,1)S(1)}, u32[]{:S(2)}, u32[]{:S(2)}) collective-permute-start(bf16[64,1024]{1,0:T(8,128)(2,1)S(1)} %pad_maximum_fusion.19), channel_id=1, source_target_pairs={{0,6},{1,7},{2,0},{3,1},{4,2},{5,3},{6,4},{7,5},{8,14},{9,15},{10,... | collective-permute-start | bytes 393224 | tf_op jit(solution)/shard_map/ppermute | solution.py:15
  435.5 10.7 %collective-permute-start.22 = (bf16[64,1024]{1,0:T(8,128)(2,1)S(1)}, bf16[64,1024]{1,0:T(8,128)(2,1)S(1)}, u32[]{:S(2)}, u32[]{:S(2)}) collective-permute-start(bf16[64,1024]{1,0:T(8,128)(2,1)S(1)} %pad_maximum_fusion.20), channel_id=1, source_target_pairs={{0,6},{1,7},{2,0},{3,1},{4,2},{5,3},{6,4},{7,5},{8,14},{9,15},{10,... | collective-permute-start | bytes 393224 | tf_op jit(solution)/shard_map/ppermute | solution.py:15
  438.7 36.7 %collective-permute-start.14 = (bf16[128,1024]{1,0:T(8,128)(2,1)S(1)}, bf16[128,1024]{1,0:T(8,128)(2,1)S(1)}, u32[]{:S(2)}, u32[]{:S(2)}) collective-permute-start(bf16[128,1024]{1,0:T(8,128)(2,1)S(1)} %pad_maximum_fusion.9), channel_id=1, source_target_pairs={{0,4},{1,5},{2,6},{3,7},{4,0},{5,1},{6,2},{7,3},{8,12},{9,13},{10,... | collective-permute-start | bytes 786440 | tf_op jit(solution)/shard_map/ppermute | solution.py:15
  441.5 39.5 %collective-permute-start.17 = (bf16[128,1024]{1,0:T(8,128)(2,1)S(1)}, bf16[128,1024]{1,0:T(8,128)(2,1)S(1)}, u32[]{:S(2)}, u32[]{:S(2)}) collective-permute-start(bf16[128,1024]{1,0:T(8,128)(2,1)S(1)} %pad_maximum_fusion.10), channel_id=1, source_target_pairs={{0,4},{1,5},{2,6},{3,7},{4,0},{5,1},{6,2},{7,3},{8,12},{9,13},{10,... | collective-permute-start | bytes 786440 | tf_op jit(solution)/shard_map/ppermute | solution.py:15
  444.2 42.4 %collective-permute-start.20 = (bf16[128,1024]{1,0:T(8,128)(2,1)S(1)}, bf16[128,1024]{1,0:T(8,128)(2,1)S(1)}, u32[]{:S(2)}, u32[]{:S(2)}) collective-permute-start(bf16[128,1024]{1,0:T(8,128)(2,1)S(1)} %pad_maximum_fusion.11), channel_id=1, source_target_pairs={{0,4},{1,5},{2,6},{3,7},{4,0},{5,1},{6,2},{7,3},{8,12},{9,13},{10,... | collective-permute-start | bytes 786440 | tf_op jit(solution)/shard_map/ppermute | solution.py:15
  446.3 44.7 %collective-permute-start.23 = (bf16[128,1024]{1,0:T(8,128)(2,1)S(1)}, bf16[128,1024]{1,0:T(8,128)(2,1)S(1)}, u32[]{:S(2)}, u32[]{:S(2)}) collective-permute-start(bf16[128,1024]{1,0:T(8,128)(2,1)S(1)} %pad_maximum_fusion.12), channel_id=1, source_target_pairs={{0,4},{1,5},{2,6},{3,7},{4,0},{5,1},{6,2},{7,3},{8,12},{9,13},{10,... | collective-permute-start | bytes 786440 | tf_op jit(solution)/shard_map/ppermute | solution.py:15
Sparse Core Ops, SparseCore 0:
  8.9 19.4 all-gather.1
  42.4 95.3 reduce-scatter.4
  242.8 31.8 reduce-scatter.6
  301.8 95.7 reduce-scatter.8
  503.1 31.7 reduce-scatter.10
